TPU v7x, 512 devices: a whole 4x8x8 slice. The times are simulated.
512 devices in a mesh: inp: 64 (over y_lo, z, x), tm: 8 (over y_hi, core).
Axes of the slice: x: 4, y: 8 (y_hi: 4, y_lo: 2; y = y_hi * 2 + y_lo), z: 8, core: 2. Of those that a mesh axis runs over, the one named last changes fastest.
Arguments:
- samples: bfloat16 [1024, 64, 1024], P('inp', 'tm'), may hold values from -8 to 8
- filter_taps: float32 [4, 1024], replicated, may hold values from -0.09375 to 0.09375
- partner_mask: int32 [2], replicated, may hold values from 1 to 63, as said below
Outputs:
- visibilities: float32 [1024, 3, 16, 1024], P('inp', None, None, 'tm')
Inputs may be any that keep to these rules, and one draw needn't show every extreme that they name: `partner_mask`: the 2 masks are distinct and one of them is 63; in a round, input block p pairs with input block p XOR the mask.
All inputs are finite; a program needn't handle non-finite values.
Results may differ from a plain program's by a relative error of at most 0.0009.
Values may be sent and summed in bfloat16 or wider, within the bound.
No kernel may reach another device: no remote copies, remote signals or barrier semaphores. Data moves between devices by JAX's collectives and lax.ppermute only.
A program may use at most 64 MiB of HBM per device.

v0:
```python
import math

import jax
import jax.numpy as jnp
from jax import lax
from jax.sharding import PartitionSpec as P

TAPS = 4
ROUNDS = 2


def shifted(block, axis, distance):
    devices = range(lax.axis_size(axis))
    route = [(i - distance, i) for i in devices if i - distance in devices]
    return lax.ppermute(block, axis, route)


def swapped_2(x, axis, bit):
    return lax.ppermute(x, axis, [(i, i ^ 1 << bit) for i in range(lax.axis_size(axis))])


def dft_columns(n_fft):
    channels = n_fft // 2
    sample_ids = jnp.arange(n_fft, dtype=jnp.int32)[:, None]
    chan_ids = jnp.arange(channels, dtype=jnp.int32)[None, :]
    phase = (sample_ids * chan_ids % n_fft).astype(jnp.float32) * (2.0 * math.pi / n_fft)
    return jnp.concatenate([jnp.cos(phase), -jnp.sin(phase)], axis=1)


def cross_batched(left, right):
    left_re = left[:, :, None, :, 0, :].astype(jnp.float32)
    left_im = left[:, :, None, :, 1, :].astype(jnp.float32)
    right_re = right[:, None, :, :, 0, :].astype(jnp.float32)
    right_im = right[:, None, :, :, 1, :].astype(jnp.float32)
    real_part = jnp.sum(left_re * right_re + left_im * right_im, axis=3)
    imag_part = jnp.sum(left_im * right_re - left_re * right_im, axis=3)
    return jnp.stack([real_part, imag_part], axis=-2)


def cross_single(left, right):
    return cross_batched(left[None], right[None])[0]


def channelize(samples, filter_taps):
    in_dev, spec_dev, n_fft = samples.shape
    history = shifted(samples[:, spec_dev - (TAPS - 1) :, :], "tm", 1)
    frames = jnp.concatenate([history, samples], axis=1)
    filtered = jnp.zeros((in_dev, spec_dev, n_fft), jnp.float32)
    for tap_index in range(TAPS):
        filtered = filtered + filter_taps[tap_index][None, None, :] * frames[
            :, tap_index : tap_index + spec_dev, :
        ].astype(jnp.float32)
    dft_table = dft_columns(n_fft)
    spectra = jnp.dot(
        filtered.reshape(in_dev * spec_dev, n_fft),
        dft_table,
        precision=lax.Precision.HIGHEST,
        preferred_element_type=jnp.float32,
    )
    return spectra.astype(jnp.bfloat16).reshape(in_dev, spec_dev, 2, n_fft // 2)


def on_device(samples, filter_taps, partner_mask):
    own_block = channelize(samples, filter_taps)
    in_dev, spec_dev, both_parts, channels = own_block.shape
    norm_scale = 1.0 / (spec_dev * lax.axis_size("tm"))
    bit_levels = lax.axis_size("inp").bit_length() - 1
    pair_terms = [cross_single(own_block, own_block)]
    partner = own_block
    previous = jnp.int32(0)
    for round_index in range(ROUNDS):
        round_mask = partner_mask[round_index]
        change = jnp.bitwise_xor(round_mask, previous)
        for bit_level in range(bit_levels):
            swapped = swapped_2(partner, "inp", bit_level)
            needed = jnp.bitwise_and(jnp.right_shift(change, bit_level), 1) == 1
            partner = jnp.where(needed, swapped, partner)
        pair_terms.append(cross_single(own_block, partner))
        previous = round_mask
    partial_value = jnp.stack(pair_terms, axis=1) * norm_scale
    local_terms = partial_value.reshape(in_dev, ROUNDS + 1, in_dev, 2 * channels)
    return lax.psum_scatter(local_terms, "tm", scatter_dimension=3, tiled=True)


def solution(mesh):
    in_specs = (P("inp", "tm", None), P(), P())
    out_specs = P("inp", None, None, "tm")
    return jax.shard_map(
        on_device, mesh=mesh, in_specs=in_specs, out_specs=out_specs, check_vma=False
    )
```

profile of v0, /device:TPU:1, one launch (start us, length us, event | category | flops | bytes accessed | tf_op | source)
XLA Modules:
  0.0 249.7 jit_solution(2071689450787130230)
XLA Ops:
  7.6 5.6 %collective-permute-start = (bf16[16,3,1024]{2,1,0:T(4,128)(2,1)S(1)}, bf16[16,3,1024]{2,1,0:T(4,128)(2,1)S(1)}, u32[]{:S(2)}, u32[]{:S(2)}) collective-permute-start(bf16[16,3,1024]{2,1,0:T(4,128)(2,1)S(1)} %slice.55), channel_id=1, source_target_pairs={{0,1},{1,2},{2,3},{3,4},{4,5},{5,6},{6,7},{8,9},{9,10},{10,11},{11... | collective-permute-start | bytes 294920 | tf_op jit(solution)/shard_map/ppermute | solution.py:15
  13.2 8.2 %sine_negate_fusion = (f32[1024,512]{1,0:T(8,128)S(1)}, f32[1024,512]{1,0:T(8,128)S(1)}) fusion(), kind=kLoop, calls=%fused_computation.17 | loop fusion | flops 7864320 | bytes 4194304 | tf_op jit(solution)/shard_map/neg | solution.py:27
  28.6 3.3 %collective-permute-done.1 = bf16[16,8,2,512]{3,1,2,0:T(8,128)(2,1)S(1)} collective-permute-done((bf16[16,8,2,512]{3,1,2,0:T(8,128)(2,1)S(1)}, bf16[16,8,2,512]{3,1,2,0:T(8,128)(2,1)S(1)}, u32[]{:S(2)}, u32[]{:S(2)}) %collective-permute-start.1) | collective-permute-done | bytes 262176 | tf_op jit(solution)/shard_map/ppermute | solution.py:19
  32.0 5.2 %collective-permute-start.2 = (bf16[16,8,2,512]{3,1,2,0:T(8,128)(2,1)S(1)}, bf16[16,8,2,512]{3,1,2,0:T(8,128)(2,1)S(1)}, u32[]{:S(2)}, u32[]{:S(2)}) collective-permute-start(bf16[16,8,2,512]{3,1,2,0:T(8,128)(2,1)S(1)} %broadcast_select_fusion.5), channel_id=1, source_target_pairs={{0,16},{8,24},{16,0},{24,8},{32,48},{40,56},{48,32},{56,40},{64,80... | collective-permute-start | bytes 786440 | tf_op jit(solution)/shard_map/ppermute | solution.py:19
  37.8 5.1 %collective-permute-done.2 = bf16[16,8,2,512]{3,1,2,0:T(8,128)(2,1)S(1)} collective-permute-done((bf16[16,8,2,512]{3,1,2,0:T(8,128)(2,1)S(1)}, bf16[16,8,2,512]{3,1,2,0:T(8,128)(2,1)S(1)}, u32[]{:S(2)}, u32[]{:S(2)}) %collective-permute-start.2) | collective-permute-done | bytes 262176 | tf_op jit(solution)/shard_map/ppermute | solution.py:19
  42.9 4.1 %collective-permute-start.3 = (bf16[16,8,2,512]{3,1,2,0:T(8,128)(2,1)S(1)}, bf16[16,8,2,512]{3,1,2,0:T(8,128)(2,1)S(1)}, u32[]{:S(2)}, u32[]{:S(2)}) collective-permute-start(bf16[16,8,2,512]{3,1,2,0:T(8,128)(2,1)S(1)} %broadcast_select_fusion.6), channel_id=1, source_target_pairs={{0,32},{8,40},{16,48},{24,56},{32,0},{40,8},{48,16},{56,24},{64,96... | collective-permute-start | bytes 786440 | tf_op jit(solution)/shard_map/ppermute | solution.py:19
  47.6 5.3 %collective-permute-done.3 = bf16[16,8,2,512]{3,1,2,0:T(8,128)(2,1)S(1)} collective-permute-done((bf16[16,8,2,512]{3,1,2,0:T(8,128)(2,1)S(1)}, bf16[16,8,2,512]{3,1,2,0:T(8,128)(2,1)S(1)}, u32[]{:S(2)}, u32[]{:S(2)}) %collective-permute-start.3) | collective-permute-done | bytes 262176 | tf_op jit(solution)/shard_map/ppermute | solution.py:19
  52.9 6.7 %collective-permute-start.4 = (bf16[16,8,2,512]{3,1,2,0:T(8,128)(2,1)S(1)}, bf16[16,8,2,512]{3,1,2,0:T(8,128)(2,1)S(1)}, u32[]{:S(2)}, u32[]{:S(2)}) collective-permute-start(bf16[16,8,2,512]{3,1,2,0:T(8,128)(2,1)S(1)} %broadcast_select_fusion.7), channel_id=1, source_target_pairs={{0,64},{8,72},{16,80},{24,88},{32,96},{40,104},{48,112},{56,120},{... | collective-permute-start | bytes 786440 | tf_op jit(solution)/shard_map/ppermute | solution.py:19
  60.2 11.3 %collective-permute-done.4 = bf16[16,8,2,512]{3,1,2,0:T(8,128)(2,1)S(1)} collective-permute-done((bf16[16,8,2,512]{3,1,2,0:T(8,128)(2,1)S(1)}, bf16[16,8,2,512]{3,1,2,0:T(8,128)(2,1)S(1)}, u32[]{:S(2)}, u32[]{:S(2)}) %collective-permute-start.4) | collective-permute-done | bytes 262176 | tf_op jit(solution)/shard_map/ppermute | solution.py:19
  71.5 7.8 %collective-permute-start.5 = (bf16[16,8,2,512]{3,1,2,0:T(8,128)(2,1)S(1)}, bf16[16,8,2,512]{3,1,2,0:T(8,128)(2,1)S(1)}, u32[]{:S(2)}, u32[]{:S(2)}) collective-permute-start(bf16[16,8,2,512]{3,1,2,0:T(8,128)(2,1)S(1)} %broadcast_select_fusion.8), channel_id=1, source_target_pairs={{0,128},{8,136},{16,144},{24,152},{32,160},{40,168},{48,176},{56,1... | collective-permute-start | bytes 786440 | tf_op jit(solution)/shard_map/ppermute | solution.py:19
  79.9 7.5 %collective-permute-done.5 = bf16[16,8,2,512]{3,1,2,0:T(8,128)(2,1)S(1)} collective-permute-done((bf16[16,8,2,512]{3,1,2,0:T(8,128)(2,1)S(1)}, bf16[16,8,2,512]{3,1,2,0:T(8,128)(2,1)S(1)}, u32[]{:S(2)}, u32[]{:S(2)}) %collective-permute-start.5) | collective-permute-done | bytes 262176 | tf_op jit(solution)/shard_map/ppermute | solution.py:19
  87.5 3.2 %collective-permute-start.6 = (bf16[16,8,2,512]{3,1,2,0:T(8,128)(2,1)S(1)}, bf16[16,8,2,512]{3,1,2,0:T(8,128)(2,1)S(1)}, u32[]{:S(2)}, u32[]{:S(2)}) collective-permute-start(bf16[16,8,2,512]{3,1,2,0:T(8,128)(2,1)S(1)} %broadcast_select_fusion.9), channel_id=1, source_target_pairs={{0,256},{8,264},{16,272},{24,280},{32,288},{40,296},{48,304},{56,3... | collective-permute-start | bytes 786440 | tf_op jit(solution)/shard_map/ppermute | solution.py:19
  91.3 3.3 %collective-permute-done.6 = bf16[16,8,2,512]{3,1,2,0:T(8,128)(2,1)S(1)} collective-permute-done((bf16[16,8,2,512]{3,1,2,0:T(8,128)(2,1)S(1)}, bf16[16,8,2,512]{3,1,2,0:T(8,128)(2,1)S(1)}, u32[]{:S(2)}, u32[]{:S(2)}) %collective-permute-start.6) | collective-permute-done | bytes 262176 | tf_op jit(solution)/shard_map/ppermute | solution.py:19
  101.8 4.7 %collective-permute-start.8 = (bf16[16,8,2,512]{3,1,2,0:T(8,128)(2,1)S(1)}, bf16[16,8,2,512]{3,1,2,0:T(8,128)(2,1)S(1)}, u32[]{:S(2)}, u32[]{:S(2)}) collective-permute-start(bf16[16,8,2,512]{3,1,2,0:T(8,128)(2,1)S(1)} %broadcast_select_fusion), channel_id=1, source_target_pairs={{0,16},{8,24},{16,0},{24,8},{32,48},{40,56},{48,32},{56,40},{64,80... | collective-permute-start | bytes 786440 | tf_op jit(solution)/shard_map/ppermute | solution.py:19
  106.5 6.7 %collective-permute-done.8 = bf16[16,8,2,512]{3,1,2,0:T(8,128)(2,1)S(1)} collective-permute-done((bf16[16,8,2,512]{3,1,2,0:T(8,128)(2,1)S(1)}, bf16[16,8,2,512]{3,1,2,0:T(8,128)(2,1)S(1)}, u32[]{:S(2)}, u32[]{:S(2)}) %collective-permute-start.8) | collective-permute-done | bytes 262176 | tf_op jit(solution)/shard_map/ppermute | solution.py:19
  115.9 4.5 %collective-permute-done.9 = bf16[16,8,2,512]{3,1,2,0:T(8,128)(2,1)S(1)} collective-permute-done((bf16[16,8,2,512]{3,1,2,0:T(8,128)(2,1)S(1)}, bf16[16,8,2,512]{3,1,2,0:T(8,128)(2,1)S(1)}, u32[]{:S(2)}, u32[]{:S(2)}) %collective-permute-start.9) | collective-permute-done | bytes 262176 | tf_op jit(solution)/shard_map/ppermute | solution.py:19
  120.4 7.6 %collective-permute-start.10 = (bf16[16,8,2,512]{3,1,2,0:T(8,128)(2,1)S(1)}, bf16[16,8,2,512]{3,1,2,0:T(8,128)(2,1)S(1)}, u32[]{:S(2)}, u32[]{:S(2)}) collective-permute-start(bf16[16,8,2,512]{3,1,2,0:T(8,128)(2,1)S(1)} %broadcast_select_fusion.2), channel_id=1, source_target_pairs={{0,64},{8,72},{16,80},{24,88},{32,96},{40,104},{48,112},{56,120},{... | collective-permute-start | bytes 786440 | tf_op jit(solution)/shard_map/ppermute | solution.py:19
  128.0 7.2 %collective-permute-done.10 = bf16[16,8,2,512]{3,1,2,0:T(8,128)(2,1)S(1)} collective-permute-done((bf16[16,8,2,512]{3,1,2,0:T(8,128)(2,1)S(1)}, bf16[16,8,2,512]{3,1,2,0:T(8,128)(2,1)S(1)}, u32[]{:S(2)}, u32[]{:S(2)}) %collective-permute-start.10) | collective-permute-done | bytes 262176 | tf_op jit(solution)/shard_map/ppermute | solution.py:19
  137.6 10.2 %collective-permute-done.11 = bf16[16,8,2,512]{3,1,2,0:T(8,128)(2,1)S(1)} collective-permute-done((bf16[16,8,2,512]{3,1,2,0:T(8,128)(2,1)S(1)}, bf16[16,8,2,512]{3,1,2,0:T(8,128)(2,1)S(1)}, u32[]{:S(2)}, u32[]{:S(2)}) %collective-permute-start.11) | collective-permute-done | bytes 262176 | tf_op jit(solution)/shard_map/ppermute | solution.py:19
  147.9 3.2 %collective-permute-start.12 = (bf16[16,8,2,512]{3,1,2,0:T(8,128)(2,1)S(1)}, bf16[16,8,2,512]{3,1,2,0:T(8,128)(2,1)S(1)}, u32[]{:S(2)}, u32[]{:S(2)}) collective-permute-start(bf16[16,8,2,512]{3,1,2,0:T(8,128)(2,1)S(1)} %broadcast_select_fusion.4), channel_id=1, source_target_pairs={{0,256},{8,264},{16,272},{24,280},{32,288},{40,296},{48,304},{56,3... | collective-permute-start | bytes 786440 | tf_op jit(solution)/shard_map/ppermute | solution.py:19
  151.2 4.1 %collective-permute-done.12 = bf16[16,8,2,512]{3,1,2,0:T(8,128)(2,1)S(1)} collective-permute-done((bf16[16,8,2,512]{3,1,2,0:T(8,128)(2,1)S(1)}, bf16[16,8,2,512]{3,1,2,0:T(8,128)(2,1)S(1)}, u32[]{:S(2)}, u32[]{:S(2)}) %collective-permute-start.12) | collective-permute-done | bytes 262176 | tf_op jit(solution)/shard_map/ppermute | solution.py:19
  155.4 10.2 %add_reduce_fusion.1 = (f32[16,16,512]{2,1,0:T(8,128)S(1)}, f32[16,16,512]{2,1,0:T(8,128)S(1)}, f32[16,16,512]{2,1,0:T(8,128)S(1)}, f32[16,16,512]{2,1,0:T(8,128...) fusion(f32[16,8,512]{2,1,0:T(8,128)S(1)} %get-tuple-element.20, f32[16,8,512]{2,1,0:T(8,128)S(1)} %get-tuple-element.19, ...), kind=kLoop, calls=%fused_computation.7 | loop fusion | flops 24379392 | bytes 4718592 | tf_op jit(solution)/shard_map/reduce_sum | solution.py:35
  173.3 3.3 %maximum_multiply_fusion = f32[16,3,16,1024]{3,2,0,1:T(8,128)} fusion(f32[16,1,16,1024]{3,2,0,1:T(8,128)} %stack.47, f32[16,1,16,1024]{3,2,0,1:T(8,128)S(1)} %stack.43, f32[16,1,16,1024]{3,2,0,1:T(8,128)S(1)} %stack.39), kind=kLoop, calls=%fused_computation.10 | loop fusion | flops 2359296 | bytes 6291456 | tf_op jit(solution)/shard_map/mul | solution.py:80
  176.6 64.6 %reduce-scatter.2.cloned.1.call-done = f32[16,3,16,128]{3,2,0,1:T(8,128)} async-done(((f32[16,3,16,1024]{3,2,0,1:T(8,128)}), f32[16,3,16,128]{3,2,0,1:T(8,128)}) %reduce-scatter.2.cloned.1.call-update) | async-done | bytes 393232 | tf_op jit(solution)/shard_map/reduce_scatter | solution.py:82
  (43 shorter events, 28.3 us)
Async XLA Ops:
  6.5 15.0 %copy-start = (bf16[16,8,1024]{2,1,0:T(8,128)(2,1)S(1)}, bf16[16,8,1024]{2,1,0:T(8,128)(2,1)}, u32[]{:S(2)}) copy-start(bf16[16,8,1024]{2,1,0:T(8,128)(2,1)} %param.3) | copy-start | bytes 786436
  6.5 15.0 %copy-start.1 = (f32[4,1024]{1,0:T(4,128)S(1)}, f32[4,1024]{1,0:T(4,128)}, u32[]{:S(2)}) copy-start(f32[4,1024]{1,0:T(4,128)} %param.4) | copy-start | bytes 49156
  6.5 234.6 %reduce-scatter.2.cloned.1.call-start = ((), (), s32[]{:S(2)}) async-start(), calls=%async_computation.1 | async-start | bytes 3538944 | tf_op jit(solution)/shard_map/reduce_scatter | solution.py:82
  7.6 13.9 %collective-permute-start = (bf16[16,3,1024]{2,1,0:T(4,128)(2,1)S(1)}, bf16[16,3,1024]{2,1,0:T(4,128)(2,1)S(1)}, u32[]{:S(2)}, u32[]{:S(2)}) collective-permute-start(bf16[16,3,1024]{2,1,0:T(4,128)(2,1)S(1)} %slice.55), channel_id=1, source_target_pairs={{0,1},{1,2},{2,3},{3,4},{4,5},{5,6},{6,7},{8,9},{9,10},{10,11},{11... | collective-permute-start | bytes 294920 | tf_op jit(solution)/shard_map/ppermute | solution.py:15
  21.5 5.9 %copy-start.2 = (s32[2]{0:T(128)S(1)}, s32[2]{0:T(128)}, u32[]{:S(2)}) copy-start(s32[2]{0:T(128)} %param.5) | copy-start | bytes 28
  24.3 7.6 %collective-permute-start.1 = (bf16[16,8,2,512]{3,1,2,0:T(8,128)(2,1)S(1)}, bf16[16,8,2,512]{3,1,2,0:T(8,128)(2,1)S(1)}, u32[]{:S(2)}, u32[]{:S(2)}) collective-permute-start(bf16[16,8,2,512]{3,1,2,0:T(8,128)(2,1)S(1)} %bitcast.67), channel_id=1, source_target_pairs={{0,8},{8,0},{16,24},{24,16},{32,40},{40,32},{48,56},{56,48},{64,72... | collective-permute-start | bytes 786440 | tf_op jit(solution)/shard_map/ppermute | solution.py:19
  32.0 10.9 %collective-permute-start.2 = (bf16[16,8,2,512]{3,1,2,0:T(8,128)(2,1)S(1)}, bf16[16,8,2,512]{3,1,2,0:T(8,128)(2,1)S(1)}, u32[]{:S(2)}, u32[]{:S(2)}) collective-permute-start(bf16[16,8,2,512]{3,1,2,0:T(8,128)(2,1)S(1)} %broadcast_select_fusion.5), channel_id=1, source_target_pairs={{0,16},{8,24},{16,0},{24,8},{32,48},{40,56},{48,32},{56,40},{64,80... | collective-permute-start | bytes 786440 | tf_op jit(solution)/shard_map/ppermute | solution.py:19
  42.9 10.0 %collective-permute-start.3 = (bf16[16,8,2,512]{3,1,2,0:T(8,128)(2,1)S(1)}, bf16[16,8,2,512]{3,1,2,0:T(8,128)(2,1)S(1)}, u32[]{:S(2)}, u32[]{:S(2)}) collective-permute-start(bf16[16,8,2,512]{3,1,2,0:T(8,128)(2,1)S(1)} %broadcast_select_fusion.6), channel_id=1, source_target_pairs={{0,32},{8,40},{16,48},{24,56},{32,0},{40,8},{48,16},{56,24},{64,96... | collective-permute-start | bytes 786440 | tf_op jit(solution)/shard_map/ppermute | solution.py:19
  52.9 18.6 %collective-permute-start.4 = (bf16[16,8,2,512]{3,1,2,0:T(8,128)(2,1)S(1)}, bf16[16,8,2,512]{3,1,2,0:T(8,128)(2,1)S(1)}, u32[]{:S(2)}, u32[]{:S(2)}) collective-permute-start(bf16[16,8,2,512]{3,1,2,0:T(8,128)(2,1)S(1)} %broadcast_select_fusion.7), channel_id=1, source_target_pairs={{0,64},{8,72},{16,80},{24,88},{32,96},{40,104},{48,112},{56,120},{... | collective-permute-start | bytes 786440 | tf_op jit(solution)/shard_map/ppermute | solution.py:19
  71.5 15.9 %collective-permute-start.5 = (bf16[16,8,2,512]{3,1,2,0:T(8,128)(2,1)S(1)}, bf16[16,8,2,512]{3,1,2,0:T(8,128)(2,1)S(1)}, u32[]{:S(2)}, u32[]{:S(2)}) collective-permute-start(bf16[16,8,2,512]{3,1,2,0:T(8,128)(2,1)S(1)} %broadcast_select_fusion.8), channel_id=1, source_target_pairs={{0,128},{8,136},{16,144},{24,152},{32,160},{40,168},{48,176},{56,1... | collective-permute-start | bytes 786440 | tf_op jit(solution)/shard_map/ppermute | solution.py:19
  87.5 7.1 %collective-permute-start.6 = (bf16[16,8,2,512]{3,1,2,0:T(8,128)(2,1)S(1)}, bf16[16,8,2,512]{3,1,2,0:T(8,128)(2,1)S(1)}, u32[]{:S(2)}, u32[]{:S(2)}) collective-permute-start(bf16[16,8,2,512]{3,1,2,0:T(8,128)(2,1)S(1)} %broadcast_select_fusion.9), channel_id=1, source_target_pairs={{0,256},{8,264},{16,272},{24,280},{32,288},{40,296},{48,304},{56,3... | collective-permute-start | bytes 786440 | tf_op jit(solution)/shard_map/ppermute | solution.py:19
  94.7 7.1 %collective-permute-start.7 = (bf16[16,8,2,512]{3,1,2,0:T(8,128)(2,1)S(1)}, bf16[16,8,2,512]{3,1,2,0:T(8,128)(2,1)S(1)}, u32[]{:S(2)}, u32[]{:S(2)}) collective-permute-start(bf16[16,8,2,512]{3,1,2,0:T(8,128)(2,1)S(1)} %broadcast_select_fusion.10), channel_id=1, source_target_pairs={{0,8},{8,0},{16,24},{24,16},{32,40},{40,32},{48,56},{56,48},{64,72... | collective-permute-start | bytes 786440 | tf_op jit(solution)/shard_map/ppermute | solution.py:19
  101.8 11.4 %collective-permute-start.8 = (bf16[16,8,2,512]{3,1,2,0:T(8,128)(2,1)S(1)}, bf16[16,8,2,512]{3,1,2,0:T(8,128)(2,1)S(1)}, u32[]{:S(2)}, u32[]{:S(2)}) collective-permute-start(bf16[16,8,2,512]{3,1,2,0:T(8,128)(2,1)S(1)} %broadcast_select_fusion), channel_id=1, source_target_pairs={{0,16},{8,24},{16,0},{24,8},{32,48},{40,56},{48,32},{56,40},{64,80... | collective-permute-start | bytes 786440 | tf_op jit(solution)/shard_map/ppermute | solution.py:19
  113.3 7.1 %collective-permute-start.9 = (bf16[16,8,2,512]{3,1,2,0:T(8,128)(2,1)S(1)}, bf16[16,8,2,512]{3,1,2,0:T(8,128)(2,1)S(1)}, u32[]{:S(2)}, u32[]{:S(2)}) collective-permute-start(bf16[16,8,2,512]{3,1,2,0:T(8,128)(2,1)S(1)} %broadcast_select_fusion.1), channel_id=1, source_target_pairs={{0,32},{8,40},{16,48},{24,56},{32,0},{40,8},{48,16},{56,24},{64,96... | collective-permute-start | bytes 786440 | tf_op jit(solution)/shard_map/ppermute | solution.py:19
  120.4 14.8 %collective-permute-start.10 = (bf16[16,8,2,512]{3,1,2,0:T(8,128)(2,1)S(1)}, bf16[16,8,2,512]{3,1,2,0:T(8,128)(2,1)S(1)}, u32[]{:S(2)}, u32[]{:S(2)}) collective-permute-start(bf16[16,8,2,512]{3,1,2,0:T(8,128)(2,1)S(1)} %broadcast_select_fusion.2), channel_id=1, source_target_pairs={{0,64},{8,72},{16,80},{24,88},{32,96},{40,104},{48,112},{56,120},{... | collective-permute-start | bytes 786440 | tf_op jit(solution)/shard_map/ppermute | solution.py:19
  135.3 12.6 %collective-permute-start.11 = (bf16[16,8,2,512]{3,1,2,0:T(8,128)(2,1)S(1)}, bf16[16,8,2,512]{3,1,2,0:T(8,128)(2,1)S(1)}, u32[]{:S(2)}, u32[]{:S(2)}) collective-permute-start(bf16[16,8,2,512]{3,1,2,0:T(8,128)(2,1)S(1)} %broadcast_select_fusion.3), channel_id=1, source_target_pairs={{0,128},{8,136},{16,144},{24,152},{32,160},{40,168},{48,176},{56,1... | collective-permute-start | bytes 786440 | tf_op jit(solution)/shard_map/ppermute | solution.py:19
  147.9 7.4 %collective-permute-start.12 = (bf16[16,8,2,512]{3,1,2,0:T(8,128)(2,1)S(1)}, bf16[16,8,2,512]{3,1,2,0:T(8,128)(2,1)S(1)}, u32[]{:S(2)}, u32[]{:S(2)}) collective-permute-start(bf16[16,8,2,512]{3,1,2,0:T(8,128)(2,1)S(1)} %broadcast_select_fusion.4), channel_id=1, source_target_pairs={{0,256},{8,264},{16,272},{24,280},{32,288},{40,296},{48,304},{56,3... | collective-permute-start | bytes 786440 | tf_op jit(solution)/shard_map/ppermute | solution.py:19
Sparse Core Ops, SparseCore 0:
  176.7 64.4 reduce-scatter.1
where the time goes:
time: 252 us; the launch traced here: 250 us
  waiting for transfers between devices  136 us (54%)
  starting transfers between devices  59.4 us (24%)
  other arithmetic  23.7 us (9%)
  between operations  18.3 us (7%)
  local copies, waits for them, and re-layouts  9.59 us (4%)
  matrix products  2.75 us (1%)
    ppermute x12, waiting for transfers between devices, swapped_2(): lax.ppermute(x, axis, [(i, i ^ 1 << bit) for i in range(lax.axis_size(axi...  71.5 us
    reduce_scatter x1, waiting for transfers between devices, on_device(): return lax.psum_scatter(local_terms, 'tm', scatter_dimension=3, tiled=True)  64.6 us
    ppermute x12, starting transfers between devices, swapped_2(): lax.ppermute(x, axis, [(i, i ^ 1 << bit) for i in range(lax.axis_size(axi...  53.8 us
    reduce_sum x1, other arithmetic, cross_batched(): real_part = jnp.sum(left_re * right_re + left_im * right_im, axis=3)  10.2 us
    neg x1, other arithmetic, dft_columns(): return jnp.concatenate([jnp.cos(phase), -jnp.sin(phase)], axis=1)  8.24 us
    ppermute x1, starting transfers between devices, shifted(): return lax.ppermute(block, axis, route)  5.61 us
  transfers between devices with their start and end apart: 14, of which 13 were waited for; matrix products, arithmetic and copies ran while one was open for 4% of the time, Pallas kernels for 0%

commit v1 on v0

--- a/solution.py
+++ b/solution.py
@@ -65,18 +65,20 @@
     in_dev, spec_dev, both_parts, channels = own_block.shape
     norm_scale = 1.0 / (spec_dev * lax.axis_size("tm"))
     bit_levels = lax.axis_size("inp").bit_length() - 1
+    inp_size = lax.axis_size("inp")
+    all_bits = inp_size - 1
     pair_terms = [cross_single(own_block, own_block)]
-    partner = own_block
-    previous = jnp.int32(0)
+    full_partner = lax.ppermute(own_block, "inp", [(i, i ^ all_bits) for i in range(inp_size)])
+    other_mask = jnp.where(partner_mask[0] == all_bits, partner_mask[1], partner_mask[0])
+    branches = [
+        (lambda m: lambda x: lax.ppermute(x, "inp", [(i, i ^ m) for i in range(inp_size)]))(m)
+        for m in range(1, all_bits)
+    ]
+    other_partner = lax.switch(jnp.clip(other_mask - 1, 0, all_bits - 2), branches, own_block)
     for round_index in range(ROUNDS):
-        round_mask = partner_mask[round_index]
-        change = jnp.bitwise_xor(round_mask, previous)
-        for bit_level in range(bit_levels):
-            swapped = swapped_2(partner, "inp", bit_level)
-            needed = jnp.bitwise_and(jnp.right_shift(change, bit_level), 1) == 1
-            partner = jnp.where(needed, swapped, partner)
+        is_full = partner_mask[round_index] == all_bits
+        partner = jnp.where(is_full, full_partner, other_partner)
         pair_terms.append(cross_single(own_block, partner))
-        previous = round_mask
     partial_value = jnp.stack(pair_terms, axis=1) * norm_scale
     local_terms = partial_value.reshape(in_dev, ROUNDS + 1, in_dev, 2 * channels)
     return lax.psum_scatter(local_terms, "tm", scatter_dimension=3, tiled=True)

time: 252 us -> 158 us (0.63)
  waiting for transfers between devices: 136 us -> 62.4 us
  starting transfers between devices: 59.4 us -> 38.7 us
    ppermute x12 -> x2, waiting for transfers between devices: 71.5 us -> 11.6 us  [the longest x1 11.6 us: on_device(): lax.ppermute(x, 'inp', [(i, i ^ m) for i in range(inp_size)])]
    ppermute x12 -> x2, starting transfers between devices: 53.8 us -> 33.1 us  [the longest x1 16.7 us: on_device(): lax.ppermute(x, 'inp', [(i, i ^ m) for i in range(inp_size)])]
    reduce_scatter x1, waiting for transfers between devices: 64.6 us -> 50.8 us  [on_device(): return lax.psum_scatter(local_terms, 'tm', scatter_dimension=3, tiled=True)]
  transfers between devices with their start and end apart: 14 -> 4, of which waited for: 13 -> 2; matrix products, arithmetic and copies ran while one was open for 4% -> 6% of each run, Pallas kernels for 0% -> 0%
where the time goes in v1:
time: 158 us; the launch traced here: 157 us
  waiting for transfers between devices  62.4 us (39%)
  starting transfers between devices  38.7 us (24%)
  other arithmetic  26 us (16%)
  between operations  16.2 us (10%)
  local copies, waits for them, and re-layouts  10.6 us (7%)
  matrix products  2.75 us (2%)
    reduce_scatter x1, waiting for transfers between devices, on_device(): return lax.psum_scatter(local_terms, 'tm', scatter_dimension=3, tiled=True)  50.8 us
    ppermute x1, starting transfers between devices, on_device(): lax.ppermute(x, 'inp', [(i, i ^ m) for i in range(inp_size)])  16.7 us
    ppermute x1, starting transfers between devices, on_device(): lax.ppermute(own_block, 'inp', [(i, i ^ all_bits) for i in range(inp_size)])  16.3 us
    ppermute x1, waiting for transfers between devices, on_device(): lax.ppermute(x, 'inp', [(i, i ^ m) for i in range(inp_size)])  11.6 us
    reduce_sum x1, other arithmetic, cross_batched(): real_part = jnp.sum(left_re * right_re + left_im * right_im, axis=3)  10.5 us
    neg x1, other arithmetic, dft_columns(): return jnp.concatenate([jnp.cos(phase), -jnp.sin(phase)], axis=1)  8.24 us
    ppermute x1, starting transfers between devices, shifted(): return lax.ppermute(block, axis, route)  5.61 us
    another operation x3, local copies, waits for them, and re-layouts, on_device(): partial_value = jnp.stack(pair_terms, axis=1) * norm_scale  3.68 us
  transfers between devices with their start and end apart: 4, of which 2 were waited for; matrix products, arithmetic and copies ran while one was open for 6% of the time, Pallas kernels for 0%

profile of v1, /device:TPU:1, one launch (start us, length us, event | category | flops | bytes accessed | tf_op | source)
XLA Modules:
  0.0 156.9 jit_solution(6105496910836624469)
XLA Ops:
  6.5 1.1 slice.58
  7.6 5.6 %collective-permute-start.62 = (bf16[16,3,1024]{2,1,0:T(4,128)(2,1)S(1)}, bf16[16,3,1024]{2,1,0:T(4,128)(2,1)S(1)}, u32[]{:S(2)}, u32[]{:S(2)}) collective-permute-start(bf16[16,3,1024]{2,1,0:T(4,128)(2,1)S(1)} %slice.58), channel_id=1, source_target_pairs={{0,1},{1,2},{2,3},{3,4},{4,5},{5,6},{6,7},{8,9},{9,10},{10,11},{11... | collective-permute-start | bytes 294920 | tf_op jit(solution)/shard_map/ppermute | solution.py:15
  13.2 8.2 %sine_negate_fusion = (f32[1024,512]{1,0:T(8,128)S(1)}, f32[1024,512]{1,0:T(8,128)S(1)}) fusion(), kind=kLoop, calls=%fused_computation.17 | loop fusion | flops 7864320 | bytes 4194304 | tf_op jit(solution)/shard_map/neg | solution.py:27
  21.6 2.8 %fusion.10 = bf16[128,1024]{1,0:T(8,128)(2,1)S(1)} fusion(f32[1024,512]{1,0:T(8,128)S(1)} %get-tuple-element.154, f32[1024,512]{1,0:T(8,128)S(1)} %get-tuple-element.155, bf16[16,8,1024]{2,1,0:T(8,128)(2,1)S(1)} %copy-done, bf16[16,3,1024]{2,1,0:T(4,128)(2,1)S(1)} %collective-permute-done.62, f32[1024]{0:T(1024)S(1)} %bitcast.57, f32[1024]{0:T(1024)S(1)} %bitcast.58, ...), kind=kOutput, calls=%fused_computation.21 | convolution fusion | flops 1614413824 | bytes 4833280 | tf_op jit(solution)/shard_map/dot_general | solution.py:54
  24.3 0.9 copy.131
  25.2 16.3 %collective-permute-start.63 = (bf16[16,8,2,512]{3,2,1,0:T(2,128)(2,1)}, bf16[16,8,2,512]{3,2,1,0:T(2,128)(2,1)S(1)}, u32[]{:S(2)}, u32[]{:S(2)}) collective-permute-start(bf16[16,8,2,512]{3,2,1,0:T(2,128)(2,1)} %copy.131), channel_id=1, source_target_pairs={{0,504},{8,496},{16,488},{24,480},{32,472},{40,464},{48,456},{56,4... | collective-permute-start | bytes 786440 | tf_op jit(solution)/shard_map/ppermute | solution.py:71
  41.6 0.6 fusion.42
  44.9 28.5 %conditional.1 = (bf16[16,8,2,512]{3,2,1,0:T(2,128)(2,1)}) conditional(s32[]{:T(128)} %clamp.3, bf16[16,8,2,512]{3,2,1,0:T(2,128)(2,1)} %copy.131, bf16[16,8,2,512]{3,2,1,0:T(2,128)(2,1)} %copy.131, bf16[16,8,2,512]{3,2,1,0:T(2,128)(2,1)} %copy.131, bf16[16,8,2,512]{3,2,1,0:T(2,128)(2,1)} %copy.131, ...), branch_computations={%region_2.3_spmd, %region_3.4_spmd, %region_4.5_spmd, %region_5.6_... | conditional | bytes 1048624 | solution.py:77
  45.1 16.7 %collective-permute-start.38 = (bf16[16,8,2,512]{3,2,1,0:T(2,128)(2,1)}, bf16[16,8,2,512]{3,2,1,0:T(2,128)(2,1)}, u32[]{:S(2)}, u32[]{:S(2)}) collective-permute-start(bf16[16,8,2,512]{3,2,1,0:T(2,128)(2,1)} %param.38), channel_id=1, source_target_pairs={{0,312},{8,304},{16,296},{24,288},{32,280},{40,272},{48,264},{56,2... | collective-permute-start | bytes 786440 | tf_op jit(solution)/shard_map/cond/branch_38_fun/ppermute | solution.py:74
  61.8 11.6 %collective-permute-done.38 = bf16[16,8,2,512]{3,2,1,0:T(2,128)(2,1)} collective-permute-done((bf16[16,8,2,512]{3,2,1,0:T(2,128)(2,1)}, bf16[16,8,2,512]{3,2,1,0:T(2,128)(2,1)}, u32[]{:S(2)}, u32[]{:S(2)}) %collective-permute-start.38) | collective-permute-done | bytes 262176 | tf_op jit(solution)/shard_map/cond/branch_38_fun/ppermute | solution.py:74
  73.5 1.4 fusion.27
  74.9 0.5 slice_convert_fusion.1
  75.5 0.5 slice_convert_fusion.3
  76.1 10.5 %add_reduce_fusion.1 = (f32[16,16,512]{2,1,0:T(8,128)S(1)}, f32[16,16,512]{2,1,0:T(8,128)S(1)}, f32[16,16,512]{2,1,0:T(8,128)S(1)}, f32[16,16,512]{2,1,0:T(8,128...) fusion(f32[16,8,512]{2,1,0:T(8,128)S(1)} %bitcast.54, f32[16,8,512]{2,1,0:T(8,128)S(1)} %bitcast.53, ...), kind=kLoop, calls=%fused_computation.7 | loop fusion | flops 24379392 | bytes 4718592 | tf_op jit(solution)/shard_map/reduce_sum | solution.py:35
  86.7 0.8 copy.194
  87.5 0.9 stack.43
  88.5 0.8 copy.130
  89.3 0.9 stack.39
  90.2 1.3 pad_maximum_fusion.2
  91.5 0.8 copy.195
  92.3 1.9 %stack.47 = f32[16,1,16,1024]{3,2,0,1:T(8,128)} reshape(f32[1,16,16,2,512]{4,3,2,1,0:T(2,128)S(1)} %copy.195) | data formatting | bytes 2097152 | tf_op jit(solution)/shard_map/stack | solution.py:82
  94.2 3.2 %maximum_multiply_fusion = f32[16,3,16,1024]{3,2,0,1:T(8,128)} fusion(f32[16,1,16,1024]{3,2,0,1:T(8,128)} %stack.47, f32[16,1,16,1024]{3,2,0,1:T(8,128)S(1)} %stack.43, f32[16,1,16,1024]{3,2,0,1:T(8,128)S(1)} %stack.39), kind=kLoop, calls=%fused_computation.10 | loop fusion | flops 2359296 | bytes 6291456 | tf_op jit(solution)/shard_map/mul | solution.py:82
  97.5 50.8 %reduce-scatter.2.cloned.1.call-done = f32[16,3,16,128]{3,2,0,1:T(8,128)} async-done(((f32[16,3,16,1024]{3,2,0,1:T(8,128)}), f32[16,3,16,128]{3,2,0,1:T(8,128)}) %reduce-scatter.2.cloned.1.call-update) | async-done | bytes 393232 | tf_op jit(solution)/shard_map/reduce_scatter | solution.py:84
  148.3 1.8 %copy.196 = f32[16,3,16,128]{3,2,1,0:T(8,128)} copy(f32[16,3,16,128]{3,2,0,1:T(8,128)} %reduce-scatter.2.cloned.1.call-done) | data formatting | bytes 786432 | tf_op jit(solution)/shard_map/reduce_scatter | solution.py:84
  (18 shorter events, 0.3 us)
Async XLA Ops:
  6.5 15.0 %copy-start = (bf16[16,8,1024]{2,1,0:T(8,128)(2,1)S(1)}, bf16[16,8,1024]{2,1,0:T(8,128)(2,1)}, u32[]{:S(2)}) copy-start(bf16[16,8,1024]{2,1,0:T(8,128)(2,1)} %param.65) | copy-start | bytes 786436
  6.5 15.0 %copy-start.1 = (f32[4,1024]{1,0:T(4,128)S(1)}, f32[4,1024]{1,0:T(4,128)}, u32[]{:S(2)}) copy-start(f32[4,1024]{1,0:T(4,128)} %param.66) | copy-start | bytes 49156
  6.5 141.7 %reduce-scatter.2.cloned.1.call-start = ((), (), s32[]{:S(2)}) async-start(), calls=%async_computation.1 | async-start | bytes 3538944 | tf_op jit(solution)/shard_map/reduce_scatter | solution.py:84
  7.6 13.9 %collective-permute-start.62 = (bf16[16,3,1024]{2,1,0:T(4,128)(2,1)S(1)}, bf16[16,3,1024]{2,1,0:T(4,128)(2,1)S(1)}, u32[]{:S(2)}, u32[]{:S(2)}) collective-permute-start(bf16[16,3,1024]{2,1,0:T(4,128)(2,1)S(1)} %slice.58), channel_id=1, source_target_pairs={{0,1},{1,2},{2,3},{3,4},{4,5},{5,6},{6,7},{8,9},{9,10},{10,11},{11... | collective-permute-start | bytes 294920 | tf_op jit(solution)/shard_map/ppermute | solution.py:15
  21.5 20.1 %copy-start.2 = (s32[2]{0:T(128)S(1)}, s32[2]{0:T(128)}, u32[]{:S(2)}) copy-start(s32[2]{0:T(128)} %param.67) | copy-start | bytes 28
  25.2 48.2 %collective-permute-start.63 = (bf16[16,8,2,512]{3,2,1,0:T(2,128)(2,1)}, bf16[16,8,2,512]{3,2,1,0:T(2,128)(2,1)S(1)}, u32[]{:S(2)}, u32[]{:S(2)}) collective-permute-start(bf16[16,8,2,512]{3,2,1,0:T(2,128)(2,1)} %copy.131), channel_id=1, source_target_pairs={{0,504},{8,496},{16,488},{24,480},{32,472},{40,464},{48,456},{56,4... | collective-permute-start | bytes 786440 | tf_op jit(solution)/shard_map/ppermute | solution.py:71
  45.1 28.3 %collective-permute-start.38 = (bf16[16,8,2,512]{3,2,1,0:T(2,128)(2,1)}, bf16[16,8,2,512]{3,2,1,0:T(2,128)(2,1)}, u32[]{:S(2)}, u32[]{:S(2)}) collective-permute-start(bf16[16,8,2,512]{3,2,1,0:T(2,128)(2,1)} %param.38), channel_id=1, source_target_pairs={{0,312},{8,304},{16,296},{24,288},{32,280},{40,272},{48,264},{56,2... | collective-permute-start | bytes 786440 | tf_op jit(solution)/shard_map/cond/branch_38_fun/ppermute | solution.py:74
Sparse Core Ops, SparseCore 0:
  97.6 50.6 reduce-scatter.1
